TPU v7x, 256 devices: a whole 4x4x8 slice. The times are simulated.
256 devices in a mesh: batch: 8 (over x, core), tensor: 32 (over y, z).
Axes of the slice: x: 4, y: 4, z: 8, core: 2. Of those that a mesh axis runs over, the one named last changes fastest.
Arguments:
- inputs: bfloat16 [4, 8, 32, 4096], P(None, 'batch', 'tensor'), may hold values from -6 to 6
- norm_gain: float32 [4096], replicated, may hold values from 0.5 to 1.5
- norm_bias: float32 [4096], replicated, may hold values from -3 to 3
- qkv_weight: bfloat16 [4096, 3, 4096], P(None, None, 'tensor'), may hold values from -0.09375 to 0.09375
- out_weight: bfloat16 [4096, 4096], P('tensor'), may hold values from -0.375 to 0.375
- in_weight: bfloat16 [4096, 8192], P(None, 'tensor'), may hold values from -0.09375 to 0.09375
- in_bias: float32 [8192], P('tensor'), may hold values from -3 to 3
- down_weight: bfloat16 [8192, 4096], P('tensor'), may hold values from -0.0625 to 0.0625
- down_bias: float32 [4096], replicated, may hold values from -3 to 3
- page_pool: bfloat16 [128, 2, 128, 4096], P('batch', None, None, 'tensor'), may hold values from -103 to 103
- old_cache: bfloat16 [8, 32, 2, 64, 4096], P('batch', None, None, None, 'tensor'), may hold values from -103 to 103, as said below
- page_table: int32 [32, 4], replicated, may hold values from 0 to 127, as said below
- prompt_length: int32 [32], replicated, may hold values from 1 to 512, 8192 in all
- parents: int32 [4, 8, 32], replicated, may hold values from 0 to 7
Outputs:
- outputs: float32 [4, 8, 32, 4096], P(None, 'batch', 'tensor')
Inputs may be any that keep to these rules, and one draw needn't show every extreme that they name: `old_cache`: key and value entries of the beams' generated tokens. `page_table`: every pool page is named exactly once in the table. The pool is cut into as many equal blocks of consecutive pages as the batch axis has devices; request r names only pages of block r modulo that count.
All inputs are finite; a program needn't handle non-finite values.
Results may differ from a plain program's by a relative error of at most 0.034.
Values may be sent and summed in bfloat16 or wider, within the bound.
No kernel may reach another device: no remote copies, remote signals or barrier semaphores. Data moves between devices by JAX's collectives and lax.ppermute only.
A program may use at most 128 MiB of HBM per device.

v0:
```python
import math
import jax
import jax.numpy as jnp
from jax import lax
from jax.sharding import PartitionSpec as P

HDIM = 256
ROT = 64
BEAMS = 8
STEPS = 4
NEG_FILL = -1e30


def partner(value, axis, bit):
    return lax.ppermute(value, axis, [(i, i ^ 1 << bit) for i in range(lax.axis_size(axis))])


def joined_2(part, axis, combine):
    gathered = jax.tree.map(lambda a: lax.all_gather(a, axis), part)

    def take(source):
        return jax.tree.map(lambda a: lax.dynamic_index_in_dim(a, source, 0, False), gathered)

    return lax.fori_loop(
        1, lax.axis_size(axis), lambda source, state: combine(state, take(source)), take(0)
    )


def normalize(row_block, norm_gain, norm_bias):
    widened = row_block.astype(jnp.float32)
    center = jnp.mean(widened, axis=-1, keepdims=True)
    shifted = widened - center
    variance = jnp.mean(shifted * shifted, axis=-1, keepdims=True)
    return shifted * lax.rsqrt(variance + 1e-05) * norm_gain + norm_bias


def rotate_local(vectors, position, first_column):
    half_count = vectors.shape[-1] // 2
    doubled = (first_column + 2 * jnp.arange(half_count)) % HDIM
    exponent = doubled.astype(jnp.float32) / ROT
    frequency = jnp.where(doubled < ROT, jnp.exp(-exponent * math.log(10000.0)), 0.0)
    angles = position[:, None] * frequency[None, :]
    cosine = jnp.cos(angles)[None]
    sine_part = jnp.sin(angles)[None]
    halves = vectors.reshape(vectors.shape[:-1] + (half_count, 2))
    even_part = halves[..., 0]
    odd_part = halves[..., 1]
    turned = jnp.stack(
        [even_part * cosine - odd_part * sine_part, odd_part * cosine + even_part * sine_part],
        axis=-1,
    )
    return turned.reshape(vectors.shape)


def combine(earlier, later):
    peak_one, total_one, mixture_one = earlier
    peak_two, total_two, mixture_two = later
    peak = jnp.maximum(peak_one, peak_two)
    factor_one = jnp.exp(peak_one - peak)
    factor_two = jnp.exp(peak_two - peak)
    return (
        peak,
        total_one * factor_one + total_two * factor_two,
        mixture_one * factor_one[..., None] + mixture_two * factor_two[..., None],
    )


def partial_softmax(scores, allowed):
    masked = jnp.where(allowed, scores, NEG_FILL)
    peak = jnp.max(masked, axis=-1)
    weights = jnp.where(allowed, jnp.exp(masked - peak[..., None]), 0.0)
    return (peak, jnp.sum(weights, axis=-1), weights.astype(jnp.bfloat16))


def place_block(values, slot, slot_count, axis, fill_value):
    hit_shape = [1] * (values.ndim + 1)
    hit_shape[axis] = slot_count
    hits = (jnp.arange(slot_count) == slot).reshape(hit_shape)
    return jnp.where(hits, jnp.expand_dims(values, axis), fill_value)


def head_sum(prompt_scores, chain_scores):
    other_prompt, other_chain = partner((prompt_scores, chain_scores), "tensor", 0)
    prompt_scores = prompt_scores + other_prompt
    chain_scores = chain_scores + other_chain
    return (prompt_scores, chain_scores)


def on_device(
    inputs,
    norm_gain,
    norm_bias,
    qkv_weight,
    out_weight,
    in_weight,
    in_bias,
    down_weight,
    down_bias,
    page_pool,
    old_cache,
    page_table,
    prompt_length,
    parents,
):
    batch_index = lax.axis_index("batch")
    tensor_index = lax.axis_index("tensor")
    groups = lax.axis_size("batch")
    beam_dev = inputs.shape[1]
    model_width = inputs.shape[3]
    columns = qkv_weight.shape[2]
    requests = page_table.shape[0]
    history = old_cache.shape[3]
    prompt_span = page_table.shape[1] * page_pool.shape[2]
    heads_dev = max(columns // HDIM, 1)
    head_part = min(columns, HDIM)
    scale_factor = HDIM ** (-0.5)
    qkv_flat = qkv_weight.reshape(model_width, 3 * columns)
    first_column = tensor_index * columns
    owners = batch_index * beam_dev + jnp.arange(beam_dev)
    old_keys = old_cache[:, :, 0].reshape(beam_dev, requests, history, heads_dev, head_part)
    old_values = old_cache[:, :, 1].reshape(beam_dev, requests, history, heads_dev, head_part)
    stored_keys = jnp.zeros((beam_dev, requests, STEPS, columns), jnp.bfloat16)
    stored_values = jnp.zeros((beam_dev, requests, STEPS, columns), jnp.bfloat16)
    beam_ids = jnp.broadcast_to(jnp.arange(BEAMS)[:, None], (BEAMS, requests))
    prompt_ok = jnp.arange(prompt_span)[None, :] < prompt_length[:, None]
    whole_pool = lax.all_gather(page_pool, "batch", axis=0, tiled=True)
    page_rows = whole_pool[page_table]
    count_rows = page_table.shape[0]
    prompt_keys = page_rows[:, :, 0].reshape(count_rows, prompt_span, heads_dev, head_part)
    prompt_values = page_rows[:, :, 1].reshape(count_rows, prompt_span, heads_dev, head_part)
    outputs = []
    for step_index in range(STEPS):
        current = inputs[step_index]
        normed = normalize(current, norm_gain, norm_bias).astype(jnp.bfloat16)
        gathered_rows = lax.all_gather(normed, "tensor", axis=1, tiled=True)
        attn_part = jnp.einsum(
            "brd,dc->brc", gathered_rows, qkv_flat, preferred_element_type=jnp.float32
        )
        ffn_part = jnp.einsum(
            "brd,dc->brc", gathered_rows, in_weight, preferred_element_type=jnp.float32
        )
        projected = jnp.concatenate([attn_part, ffn_part], axis=-1)
        position = (prompt_length + history + step_index).astype(jnp.float32)
        queries = rotate_local(projected[..., :columns], position, first_column).astype(
            jnp.bfloat16
        )
        fresh_keys = rotate_local(
            projected[..., columns : 2 * columns], position, first_column
        ).astype(jnp.bfloat16)
        fresh_values = projected[..., 2 * columns : 3 * columns].astype(jnp.bfloat16)
        hidden = jax.nn.gelu(projected[..., 3 * columns :] + in_bias, approximate=True).astype(
            jnp.bfloat16
        )
        stored_keys = stored_keys.at[:, :, step_index].set(fresh_keys)
        stored_values = stored_values.at[:, :, step_index].set(fresh_values)
        queries_all = lax.all_gather(queries, "batch", axis=0, tiled=True)
        query_heads = queries_all.reshape(BEAMS, requests, heads_dev, head_part)
        own_heads = queries.reshape(beam_dev, requests, heads_dev, head_part)
        ancestry = []
        lineage = beam_ids
        for back_step in range(step_index, -1, -1):
            ancestry.append(lineage)
            lineage = jnp.take_along_axis(parents[back_step], lineage, axis=0)
        unused_steps = [jnp.full_like(beam_ids, -1)] * (STEPS - 1 - step_index)
        ancestry_all = jnp.stack(ancestry[::-1] + unused_steps, axis=-1)
        stored_k = stored_keys.reshape(beam_dev, requests, STEPS, heads_dev, head_part)
        stored_v = stored_values.reshape(beam_dev, requests, STEPS, heads_dev, head_part)
        chain_scores = (
            jnp.concatenate(
                [
                    jnp.einsum(
                        "brnd,jrtnd->brnjt",
                        query_heads,
                        old_keys,
                        preferred_element_type=jnp.float32,
                    ),
                    jnp.einsum(
                        "brnd,jrtnd->brnjt",
                        query_heads,
                        stored_k,
                        preferred_element_type=jnp.float32,
                    ),
                ],
                axis=-1,
            )
            * scale_factor
        )
        old_ok = jnp.broadcast_to(
            (lineage[:, :, None] == owners[None, None, :])[:, :, :, None],
            (BEAMS, requests, beam_dev, history),
        )
        new_ok = ancestry_all[:, :, None, :] == owners[None, None, :, None]
        chain_ok = jnp.concatenate([old_ok, new_ok], axis=-1)
        prompt_scores = (
            jnp.einsum(
                "brnd,rtnd->brnt", own_heads, prompt_keys, preferred_element_type=jnp.float32
            )
            * scale_factor
        )
        prompt_scores, chain_scores = head_sum(prompt_scores, chain_scores)
        prompt_peak, prompt_total, prompt_weights = partial_softmax(
            prompt_scores, prompt_ok[None, :, None, :]
        )
        prompt_mix = jnp.einsum(
            "brnt,rtnd->brnd", prompt_weights, prompt_values, preferred_element_type=jnp.float32
        )
        peak_full = place_block(prompt_peak, batch_index, groups, 0, NEG_FILL).reshape(
            BEAMS, requests, heads_dev
        )
        total_full = place_block(prompt_total, batch_index, groups, 0, 0.0).reshape(
            BEAMS, requests, heads_dev
        )
        mix_full = place_block(prompt_mix, batch_index, groups, 0, 0.0).reshape(
            BEAMS, requests, heads_dev, head_part
        )
        chain_peak, chain_total, chain_weights = partial_softmax(
            chain_scores.reshape(BEAMS, requests, heads_dev, -1), chain_ok
        )
        chain_weights = chain_weights.reshape(BEAMS, requests, heads_dev, beam_dev, history + STEPS)
        chain_mix = jnp.einsum(
            "brnjt,jrtnd->brnd",
            chain_weights[..., :history],
            old_values,
            preferred_element_type=jnp.float32,
        )
        chain_mix = chain_mix + jnp.einsum(
            "brnjt,jrtnd->brnd",
            chain_weights[..., history:],
            stored_v,
            preferred_element_type=jnp.float32,
        )
        joined = combine((peak_full, total_full, mix_full), (chain_peak, chain_total, chain_mix))
        merged = joined_2((joined[0], joined[1], joined[2]), "batch", combine)
        first_beam = batch_index * beam_dev
        total_own = lax.dynamic_slice_in_dim(merged[1], first_beam, beam_dev, 0)
        mix_own = lax.dynamic_slice_in_dim(merged[2], first_beam, beam_dev, 0)
        attention = (
            (mix_own / total_own[..., None])
            .reshape(beam_dev, requests, columns)
            .astype(jnp.bfloat16)
        )
        summed = lax.psum_scatter(
            jnp.einsum("brc,cd->rbd", attention, out_weight, preferred_element_type=jnp.float32)
            + jnp.einsum("brf,fd->rbd", hidden, down_weight, preferred_element_type=jnp.float32),
            "tensor",
            scatter_dimension=0,
            tiled=True,
        )
        update = jnp.transpose(summed, (1, 0, 2))
        result = current.astype(jnp.float32) + update + down_bias
        outputs.append(result)
    return jnp.stack(outputs, axis=0)


def solution(mesh):
    in_specs = (
        P(None, "batch", "tensor", None),
        P(),
        P(),
        P(None, None, "tensor"),
        P("tensor", None),
        P(None, "tensor"),
        P("tensor"),
        P("tensor", None),
        P(),
        P("batch", None, None, "tensor"),
        P("batch", None, None, None, "tensor"),
        P(),
        P(),
        P(),
    )
    out_specs = P(None, "batch", "tensor", None)
    return jax.shard_map(
        on_device, mesh=mesh, in_specs=in_specs, out_specs=out_specs, check_vma=False
    )
```

profile of v0, /device:TPU:2, one launch (start us, length us, event | category | flops | bytes accessed | tf_op | source)
XLA Modules:
  0.0 820.2 jit_solution(18254087234877689215)
XLA Ops:
  17.8 52.7 %all-gather.4 = bf16[131072]{0:T(1024)(128)(2,1)S(1)} all-gather(bf16[4096]{0:T(1024)(128)(2,1)S(1)} %get-tuple-element.1398), channel_id=6, replica_groups=mesh['batch'=8,'tensor'=32] {'tensor'}, dimensions={0}, use_global_device_ids=true | all-gather | bytes 270336 | tf_op jit(solution)/shard_map/all_gather | solution.py:135
  70.6 48.3 %all-gather.2 = bf16[131072]{0:T(1024)(128)(2,1)S(1)} all-gather(bf16[4096]{0:T(1024)(128)(2,1)S(1)} %get-tuple-element.1399), channel_id=4, replica_groups=mesh['batch'=8,'tensor'=32] {'tensor'}, dimensions={0}, use_global_device_ids=true | all-gather | bytes 270336 | tf_op jit(solution)/shard_map/all_gather | solution.py:135
  119.0 47.0 %all-gather = bf16[131072]{0:T(1024)(128)(2,1)S(1)} all-gather(bf16[4096]{0:T(1024)(128)(2,1)S(1)} %get-tuple-element.1400), channel_id=2, replica_groups=mesh['batch'=8,'tensor'=32] {'tensor'}, dimensions={0}, use_global_device_ids=true | all-gather | bytes 270336 | tf_op jit(solution)/shard_map/all_gather | solution.py:135
  166.8 48.2 %all-gather.6 = bf16[131072]{0:T(1024)(128)(2,1)S(1)} all-gather(bf16[4096]{0:T(1024)(128)(2,1)S(1)} %get-tuple-element.1401), channel_id=8, replica_groups=mesh['batch'=8,'tensor'=32] {'tensor'}, dimensions={0}, use_global_device_ids=true | all-gather | bytes 270336 | tf_op jit(solution)/shard_map/all_gather | solution.py:135
  215.2 4.8 copy.1379
  278.8 12.8 %all_gather.91 = bf16[8,32,128]{2,1,0:T(8,128)(2,1)S(1)} all-gather(bf16[1,32,128]{2,1,0:T(8,128)(2,1)S(1)} %copy.1416), channel_id=1, replica_groups=mesh['batch'=8,'tensor'=32] {'batch'}, dimensions={0}, use_global_device_ids=true | all-gather | bytes 73728 | tf_op jit(solution)/shard_map/all_gather | solution.py:156
  293.2 13.0 %all_gather.97 = bf16[8,32,128]{2,1,0:T(8,128)(2,1)S(1)} all-gather(bf16[1,32,128]{2,1,0:T(8,128)(2,1)} %copy.1443), channel_id=1, replica_groups=mesh['batch'=8,'tensor'=32] {'batch'}, dimensions={0}, use_global_device_ids=true | all-gather | bytes 73728 | tf_op jit(solution)/shard_map/all_gather | solution.py:156
  307.7 13.1 %all_gather.103 = bf16[8,32,128]{2,1,0:T(8,128)(2,1)S(1)} all-gather(bf16[1,32,128]{2,1,0:T(8,128)(2,1)} %copy.1470), channel_id=1, replica_groups=mesh['batch'=8,'tensor'=32] {'batch'}, dimensions={0}, use_global_device_ids=true | all-gather | bytes 73728 | tf_op jit(solution)/shard_map/all_gather | solution.py:156
  329.5 12.8 %all_gather.85 = bf16[8,32,128]{2,1,0:T(8,128)(2,1)S(1)} all-gather(bf16[1,32,128]{2,1,0:T(8,128)(2,1)S(1)} %copy.1387), channel_id=1, replica_groups=mesh['batch'=8,'tensor'=32] {'batch'}, dimensions={0}, use_global_device_ids=true | all-gather | bytes 73728 | tf_op jit(solution)/shard_map/all_gather | solution.py:156
  396.3 10.0 %gather_fusion = bf16[128,2,128,128]{3,2,1,0:T(8,128)(2,1)} fusion(bf16[128,2,128,128]{3,2,1,0:T(8,128)(2,1)} %all-gather.14.cloned.1.call-done, s32[1024]{0:T(1024)S(1)} %pad_clamp_fusion), kind=kCustom, calls=%fused_computation.10 | custom fusion | bytes 16777728 | tf_op jit(solution)/shard_map/gather | solution.py:127
  406.3 4.0 fusion.287
  465.0 12.9 %all_gather.87 = f32[8,8,32,1]{2,1,3,0:T(8,128)S(1)} all-gather(f32[1,8,32,1]{2,1,3,0:T(8,128)S(1)} %get-tuple-element.1418), channel_id=1, replica_groups=mesh['batch'=8,'tensor'=32] {'batch'}, dimensions={0}, use_global_device_ids=true | all-gather | bytes 9216 | tf_op jit(solution)/shard_map/all_gather | solution.py:19
  477.9 12.9 %all_gather.86 = f32[8,8,32,1]{2,1,3,0:T(8,128)S(1)} all-gather(f32[1,8,32,1]{2,1,3,0:T(8,128)S(1)} %get-tuple-element.1419), channel_id=1, replica_groups=mesh['batch'=8,'tensor'=32] {'batch'}, dimensions={0}, use_global_device_ids=true | all-gather | bytes 9216 | tf_op jit(solution)/shard_map/all_gather | solution.py:19
  490.8 12.9 %all_gather.104 = f32[8,8,32,1]{2,1,3,0:T(8,128)S(1)} all-gather(f32[1,8,32,1]{2,1,3,0:T(8,128)S(1)} %get-tuple-element.1443), channel_id=1, replica_groups=mesh['batch'=8,'tensor'=32] {'batch'}, dimensions={0}, use_global_device_ids=true | all-gather | bytes 9216 | tf_op jit(solution)/shard_map/all_gather | solution.py:19
  503.7 13.1 %all_gather.105 = f32[8,8,32,1]{2,1,3,0:T(8,128)S(1)} all-gather(f32[1,8,32,1]{2,1,3,0:T(8,128)S(1)} %get-tuple-element.1444), channel_id=1, replica_groups=mesh['batch'=8,'tensor'=32] {'batch'}, dimensions={0}, use_global_device_ids=true | all-gather | bytes 9216 | tf_op jit(solution)/shard_map/all_gather | solution.py:19
  516.8 12.9 %all_gather.98 = f32[8,8,32,1]{2,1,3,0:T(8,128)S(1)} all-gather(f32[1,8,32,1]{2,1,3,0:T(8,128)S(1)} %get-tuple-element.1445), channel_id=1, replica_groups=mesh['batch'=8,'tensor'=32] {'batch'}, dimensions={0}, use_global_device_ids=true | all-gather | bytes 9216 | tf_op jit(solution)/shard_map/all_gather | solution.py:19
  529.6 12.9 %all_gather.99 = f32[8,8,32,1]{2,1,3,0:T(8,128)S(1)} all-gather(f32[1,8,32,1]{2,1,3,0:T(8,128)S(1)} %get-tuple-element.1446), channel_id=1, replica_groups=mesh['batch'=8,'tensor'=32] {'batch'}, dimensions={0}, use_global_device_ids=true | all-gather | bytes 9216 | tf_op jit(solution)/shard_map/all_gather | solution.py:19
  542.5 12.9 %all_gather.92 = f32[8,8,32,1]{2,1,3,0:T(8,128)S(1)} all-gather(f32[1,8,32,1]{2,1,3,0:T(8,128)S(1)} %get-tuple-element.1447), channel_id=1, replica_groups=mesh['batch'=8,'tensor'=32] {'batch'}, dimensions={0}, use_global_device_ids=true | all-gather | bytes 9216 | tf_op jit(solution)/shard_map/all_gather | solution.py:19
  555.3 12.9 %all_gather.93 = f32[8,8,32,1]{2,1,3,0:T(8,128)S(1)} all-gather(f32[1,8,32,1]{2,1,3,0:T(8,128)S(1)} %get-tuple-element.1448), channel_id=1, replica_groups=mesh['batch'=8,'tensor'=32] {'batch'}, dimensions={0}, use_global_device_ids=true | all-gather | bytes 9216 | tf_op jit(solution)/shard_map/all_gather | solution.py:19
  573.9 16.4 %while.84 = (s32[]{:T(128)}, f32[8,32,1]{1,2,0:T(1,128)S(1)}, f32[8,32,1]{1,2,0:T(1,128)S(1)}, f32[8,32,1,128]{3,2,1,0:T(1,128)S(1)}, f32[8,8,32,1]{2,1,3,0:T(8,...) while((s32[]{:T(128)}, f32[8,32,1]{1,2,0:T(1,128)S(1)}, ...), condition=%wide.region_7.9_spmd, body=%wide.region_6.8_spmd.sunk | while | flops 99845 | bytes 931983 | solution.py:24
  591.4 11.7 %while.85 = (s32[]{:T(128)}, f32[8,32,1]{1,2,0:T(1,128)S(1)}, f32[8,32,1]{1,2,0:T(1,128)S(1)}, f32[8,32,1,128]{3,2,1,0:T(1,128)S(1)}, f32[8,8,32,1]{2,1,3,0:T(8,...) while((s32[]{:T(128)}, f32[8,32,1]{1,2,0:T(1,128)S(1)}, ...), condition=%wide.region_16.18_spmd, body=%wide.region_15.17_spmd.sunk | while | flops 99845 | bytes 931983 | solution.py:24
  604.3 16.4 %while.87 = (s32[]{:T(128)}, f32[8,32,1]{1,2,0:T(1,128)S(1)}, f32[8,32,1]{1,2,0:T(1,128)S(1)}, f32[8,32,1,128]{3,2,1,0:T(1,128)S(1)}, f32[8,8,32,1]{2,1,3,0:T(8,...) while((s32[]{:T(128)}, f32[8,32,1]{1,2,0:T(1,128)S(1)}, ...), condition=%wide.region_34.36_spmd, body=%wide.region_33.35_spmd.sunk | while | flops 99845 | bytes 931983 | solution.py:24
  624.2 26.7 %while.86 = (s32[]{:T(128)}, f32[8,32,1]{1,2,0:T(1,128)S(1)}, f32[8,32,1]{1,2,0:T(1,128)S(1)}, f32[8,32,1,128]{3,2,1,0:T(1,128)}, f32[8,8,32,1]{2,1,3,0:T(8,128)...) while((s32[]{:T(128)}, f32[8,32,1]{1,2,0:T(1,128)S(1)}, ...), condition=%wide.region_25.27_spmd, body=%wide.region_24.26_spmd.sunk | while | flops 99845 | bytes 931983 | solution.py:24
  659.1 151.5 %all-reduce.9.cloned.1.call-done = (f32[32,1,4096]{2,0,1:T(8,128)}, f32[32,1,4096]{2,0,1:T(8,128)}, f32[32,1,4096]{2,0,1:T(8,128)}, f32[32,1,4096]{2,0,1:T(8,128)}) async-done(((f32[32,1,4096]{2,0,1:T(8,128)}, f32[32,1,4096]{2,0,1:T(8,128)}, f32[32,1,4096]{2,0,1:T(8,128)}, f32[32,1,4096]{2,0,1:T(8,128)}), (f32[32,1,4096]{2,0,1:T(8,128)}, f32[32,1,4096]{2,0,1:T(8,128)}, f32[32,1,4096]{2,0,1:T(8,128)}, ...) | async-done | bytes 2097168
  (573 shorter events, 277.7 us)
Async XLA Ops:
  6.5 421.4 %copy-start = (bf16[256,4096]{1,0:T(8,128)(2,1)S(1)}, bf16[256,4096]{1,0:T(8,128)(2,1)}, u32[]{:S(2)}) copy-start(bf16[256,4096]{1,0:T(8,128)(2,1)} %param.47) | copy-start | bytes 6291460
  6.5 389.8 %all-gather.14.cloned.1.call-start = ((), (), s32[]{:S(2)}) async-start(), calls=%async_computation | async-start | bytes 9437184 | tf_op jit(solution)/shard_map/all_gather | solution.py:126
  7.3 565.5 %all-gather.16.cloned.1.call-start = ((), (), s32[]{:S(2)}) async-start(), calls=%async_computation.1 | async-start | bytes 1179648 | tf_op jit(solution)/shard_map/all_gather | solution.py:19
  119.0 110.6 %copy-start.4 = (bf16[32,4096]{1,0:T(8,128)(2,1)}, bf16[32,4096]{1,0:T(8,128)(2,1)S(1)}, u32[]{:S(2)}) copy-start(bf16[32,4096]{1,0:T(8,128)(2,1)S(1)} %reshape.3902) | copy-start | bytes 786436
  234.6 86.4 %copy-start.3 = (bf16[1,32,2,64,128]{4,3,2,1,0:T(8,128)(2,1)S(1)}, bf16[1,32,2,64,128]{4,3,2,1,0:T(8,128)(2,1)}, u32[]{:S(2)}) copy-start(bf16[1,32,2,64,128]{4,3,2,1,0:T(8,128)(2,1)} %param.50) | copy-start | bytes 3145732
  270.6 75.8 %copy-start.68 = (s32[32,4]{0,1:T(4,128)S(1)}, s32[32,4]{0,1:T(4,128)}, u32[]{:S(2)}) copy-start(s32[32,4]{0,1:T(4,128)} %param.51) | copy-start | bytes 1540
  307.7 39.4 %copy-start.56 = (s32[4,8,32]{2,1,0:T(8,128)S(1)}, s32[4,8,32]{2,1,0:T(8,128)}, u32[]{:S(2)}) copy-start(s32[4,8,32]{2,1,0:T(8,128)} %param.53) | copy-start | bytes 12292
  322.2 64.8 %collective-permute-start.7 = (f32[8,32,1,1,68]{4,0,1,3,2:T(8,128)}, f32[8,32,1,1,68]{4,0,1,3,2:T(8,128)}, u32[]{:S(2)}, u32[]{:S(2)}) collective-permute-start(f32[8,32,1,1,68]{4,0,1,3,2:T(8,128)} %maximum_multiply_fusion.3), channel_id=1, source_target_pairs={{0,1},{1,0},{2,3},{3,2},{4,5},{5,4},{6,7},{7,6},{8,9},{9,8},{10,11... | collective-permute-start | bytes 208904 | tf_op jit(solution)/shard_map/ppermute | solution.py:15
  325.5 63.4 %collective-permute-start.5 = (f32[8,32,1,1,68]{4,0,1,3,2:T(8,128)}, f32[8,32,1,1,68]{4,0,1,3,2:T(8,128)}, u32[]{:S(2)}, u32[]{:S(2)}) collective-permute-start(f32[8,32,1,1,68]{4,0,1,3,2:T(8,128)} %maximum_multiply_fusion.2), channel_id=1, source_target_pairs={{0,1},{1,0},{2,3},{3,2},{4,5},{5,4},{6,7},{7,6},{8,9},{9,8},{10,11... | collective-permute-start | bytes 208904 | tf_op jit(solution)/shard_map/ppermute | solution.py:15
  328.6 91.0 %collective-permute-start.3 = (f32[8,32,1,1,68]{4,0,1,3,2:T(8,128)}, f32[8,32,1,1,68]{4,0,1,3,2:T(8,128)}, u32[]{:S(2)}, u32[]{:S(2)}) collective-permute-start(f32[8,32,1,1,68]{4,0,1,3,2:T(8,128)} %maximum_multiply_fusion.1), channel_id=1, source_target_pairs={{0,1},{1,0},{2,3},{3,2},{4,5},{5,4},{6,7},{7,6},{8,9},{9,8},{10,11... | collective-permute-start | bytes 208904 | tf_op jit(solution)/shard_map/ppermute | solution.py:15
  343.6 47.2 %collective-permute-start.1 = (f32[8,32,1,1,68]{4,0,1,3,2:T(8,128)}, f32[8,32,1,1,68]{4,0,1,3,2:T(8,128)}, u32[]{:S(2)}, u32[]{:S(2)}) collective-permute-start(f32[8,32,1,1,68]{4,0,1,3,2:T(8,128)} %maximum_multiply_fusion), channel_id=1, source_target_pairs={{0,1},{1,0},{2,3},{3,2},{4,5},{5,4},{6,7},{7,6},{8,9},{9,8},{10,11... | collective-permute-start | bytes 208904 | tf_op jit(solution)/shard_map/ppermute | solution.py:15
  415.3 5.6 collective-permute-start.6
  415.6 6.4 collective-permute-start.4
  417.6 5.5 collective-permute-start.2
  417.7 6.1 collective-permute-start
  427.9 162.4 %all-gather.18.cloned.1.call-start = ((), (), s32[]{:S(2)}) async-start(), calls=%async_computation.2 | async-start | bytes 1179648 | tf_op jit(solution)/shard_map/all_gather | solution.py:19
  441.7 161.5 %all-gather.22.cloned.1.call-start = ((), (), s32[]{:S(2)}) async-start(), calls=%async_computation.4 | async-start | bytes 1179648 | tf_op jit(solution)/shard_map/all_gather | solution.py:19
  451.2 171.3 %all-gather.20.cloned.1.call-start = ((), (), s32[]{:S(2)}) async-start(), calls=%async_computation.3 | async-start | bytes 1179648 | tf_op jit(solution)/shard_map/all_gather | solution.py:19
  458.9 112.1 %copy-start.28 = (bf16[8,32,1,1,68]{4,0,1,3,2:T(8,128)(2,1)S(1)}, bf16[8,32,1,1,68]{4,0,1,3,2:T(8,128)(2,1)}, u32[]{:S(2)}) copy-start(bf16[8,32,1,1,68]{4,0,1,3,2:T(8,128)(2,1)} %copy-done.27) | copy-start | bytes 104452
  458.9 112.1 %copy-start.38 = (f32[32,128,8]{1,2,0:T(8,128)S(1)}, f32[32,128,8]{1,2,0:T(8,128)}, u32[]{:S(2)}) copy-start(f32[32,128,8]{1,2,0:T(8,128)} %fusion.41) | copy-start | bytes 393220
  529.6 43.2 %copy-start.35 = (f32[8,8,32,1]{2,1,3,0:T(8,128)}, f32[8,8,32,1]{2,1,3,0:T(8,128)S(1)}, u32[]{:S(2)}) copy-start(f32[8,8,32,1]{2,1,3,0:T(8,128)S(1)} %all_gather.98) | copy-start | bytes 24580
  572.7 237.9 %all-reduce.9.cloned.1.call-start = ((), (), s32[]{:S(2)}) async-start(), calls=%async_computation.5 | async-start | bytes 4194304
  655.4 155.2 %copy-start.6 = (bf16[4,1,1,4096]{3,0,2,1:T(4,128)(2,1)S(1)}, bf16[4,1,1,4096]{3,0,2,1:T(4,128)(2,1)}, u32[]{:S(2)}) copy-start(bf16[4,1,1,4096]{3,0,2,1:T(4,128)(2,1)} %param.40) | copy-start | bytes 98308
  655.4 155.2 %copy-start.57 = (f32[4096]{0:T(1024)S(1)}, f32[4096]{0:T(1024)}, u32[]{:S(2)}) copy-start(f32[4096]{0:T(1024)} %param.48) | copy-start | bytes 49156
  (63 other events, 655.4 us)
Sparse Core Ops, SparseCore 0:
  9.2 54.3 all-gather.13
  428.0 22.2 all-gather.15
  452.1 26.7 all-gather.17
  480.7 26.8 all-gather.21
  572.8 22.2 all-gather.19
  658.6 151.9 all-reduce.8
where the time goes:
time: 834 us; the launch traced here: 820 us
  blocking collectives  351 us (42%)
  waiting for transfers between devices  155 us (19%)
  local copies, waits for them, and re-layouts  150 us (18%)
  other arithmetic  73.5 us (9%)
  matrix products  59.8 us (7%)
  between operations  20.3 us (2%)
  starting transfers between devices  9 us (1%)
    all_gather x4, blocking collectives, on_device(): gathered_rows = lax.all_gather(normed, 'tensor', axis=1, tiled=True)  196 us
    unnamed x7, waiting for transfers between devices  152 us
    all_gather x8, blocking collectives, joined_2(): gathered = jax.tree.map(lambda a: lax.all_gather(a, axis), part)  103 us
    all_gather x4, blocking collectives, on_device(): queries_all = lax.all_gather(queries, 'batch', axis=0, tiled=True)  51.7 us
    dynamic_slice x98, local copies, waits for them, and re-layouts, take(): lax.dynamic_index_in_dim(a, source, 0, False)  44.8 us
    add x28, other arithmetic, combine(): mixture_one * factor_one[..., None] + mixture_two * factor_two[..., None]  29.2 us
    unnamed x160, local copies, waits for them, and re-layouts  21.6 us
  transfers between devices with their start and end apart: 14, of which 4 were waited for; matrix products, arithmetic and copies ran while one was open for 29% of the time, Pallas kernels for 0%

commit v1 on v0

--- a/solution.py
+++ b/solution.py
@@ -132,7 +132,9 @@
     for step_index in range(STEPS):
         current = inputs[step_index]
         normed = normalize(current, norm_gain, norm_bias).astype(jnp.bfloat16)
-        gathered_rows = lax.all_gather(normed, "tensor", axis=1, tiled=True)
+        gathered_rows = jnp.concatenate(
+            lax.all_to_all(jnp.stack([normed] * lax.axis_size("tensor")), "tensor", 0, 0), axis=1
+        )
         attn_part = jnp.einsum(
             "brd,dc->brc", gathered_rows, qkv_flat, preferred_element_type=jnp.float32
         )

time: 834 us -> 663 us (0.79)
  blocking collectives: 351 us -> 154 us
  starting transfers between devices: 9 us -> 40.7 us
  waiting for transfers between devices: 155 us -> 172 us
  local copies, waits for them, and re-layouts: 150 us -> 135 us
    all_gather x4 -> x0, blocking collectives: 196 us -> none  [on_device(): gathered_rows = lax.all_gather(normed, 'tensor', axis=1, tiled=True)]
    all_to_all x0 -> x4, starting transfers between devices: none -> 31.2 us  [on_device(): lax.all_to_all(jnp.stack([normed] * lax.axis_size('tensor')), 'tensor', 0...]
    all_to_all x0 -> x4, waiting for transfers between devices: none -> 15.5 us  [on_device(): lax.all_to_all(jnp.stack([normed] * lax.axis_size('tensor')), 'tensor', 0...]
    unnamed x160 -> x168, local copies, waits for them, and re-layouts: 21.6 us -> 21.6 us
    dynamic_slice x98 -> x97, local copies, waits for them, and re-layouts: 44.8 us -> 44.7 us  [take(): lax.dynamic_index_in_dim(a, source, 0, False)]
  transfers between devices with their start and end apart: 14 -> 18, of which waited for: 4 -> 7; matrix products, arithmetic and copies ran while one was open for 29% -> 34% of each run, Pallas kernels for 0% -> 0%
where the time goes in v1:
time: 663 us; the launch traced here: 655 us
  waiting for transfers between devices  172 us (26%)
  blocking collectives  154 us (23%)
  local copies, waits for them, and re-layouts  135 us (20%)
  other arithmetic  71.6 us (11%)
  matrix products  60.2 us (9%)
  starting transfers between devices  40.7 us (6%)
  between operations  20.6 us (3%)
    unnamed x7, waiting for transfers between devices  153 us
    all_gather x8, blocking collectives, joined_2(): gathered = jax.tree.map(lambda a: lax.all_gather(a, axis), part)  103 us
    all_gather x4, blocking collectives, on_device(): queries_all = lax.all_gather(queries, 'batch', axis=0, tiled=True)  51.3 us
    dynamic_slice x97, local copies, waits for them, and re-layouts, take(): lax.dynamic_index_in_dim(a, source, 0, False)  44.7 us
    all_to_all x4, starting transfers between devices, on_device(): lax.all_to_all(jnp.stack([normed] * lax.axis_size('tensor')), 'tensor', 0...  31.2 us
    add x28, other arithmetic, combine(): mixture_one * factor_one[..., None] + mixture_two * factor_two[..., None]  29.2 us
    unnamed x168, local copies, waits for them, and re-layouts  21.6 us
    gather x27, local copies, waits for them, and re-layouts, on_device(): lineage = jnp.take_along_axis(parents[back_step], lineage, axis=0)  15.6 us
  transfers between devices with their start and end apart: 18, of which 7 were waited for; matrix products, arithmetic and copies ran while one was open for 34% of the time, Pallas kernels for 0%

profile of v1, /device:TPU:2, one launch (start us, length us, event | category | flops | bytes accessed | tf_op | source)
XLA Modules:
  0.0 655.2 jit_solution(6688143017323564908)
XLA Ops:
  21.8 11.7 %all-to-all-start.3 = ((bf16[32,2,2048]{2,1,0:T(2,128)(2,1)}), bf16[32,2,2048]{2,1,0:T(2,128)(2,1)S(1)}, u32[]{:S(2)}, u32[]{:S(2)}) async-start(bf16[32,2,2048]{2,1,0:T(2,128)(2,1)} %reshape.4169), calls=%async_computation.3 | async-start | bytes 524288 | tf_op jit(solution)/shard_map/all_to_all | solution.py:136
  69.7 4.8 copy.1379
  75.7 9.9 %all-to-all-start.2 = ((bf16[32,2,2048]{2,1,0:T(2,128)(2,1)}), bf16[32,2,2048]{2,1,0:T(2,128)(2,1)S(1)}, u32[]{:S(2)}, u32[]{:S(2)}) async-start(bf16[32,2,2048]{2,1,0:T(2,128)(2,1)} %reshape.4175), calls=%async_computation.2 | async-start | bytes 524288 | tf_op jit(solution)/shard_map/all_to_all | solution.py:136
  89.7 7.8 %all-to-all-done.2 = bf16[32,2,2048]{2,1,0:T(2,128)(2,1)S(1)} async-done(((bf16[32,2,2048]{2,1,0:T(2,128)(2,1)}), bf16[32,2,2048]{2,1,0:T(2,128)(2,1)S(1)}, u32[]{:S(2)}, u32[]{:S(2)}) %all-to-all-start.2) | async-done | bytes 262176 | tf_op jit(solution)/shard_map/all_to_all | solution.py:136
  108.7 4.7 all-to-all-done.1
  114.0 5.1 all-to-all-start
  146.5 12.7 %all_gather.77 = bf16[8,32,128]{2,1,0:T(8,128)(2,1)S(1)} all-gather(bf16[1,32,128]{2,1,0:T(8,128)(2,1)S(1)} %copy.1416), channel_id=1, replica_groups=mesh['batch'=8,'tensor'=32] {'batch'}, dimensions={0}, use_global_device_ids=true | all-gather | bytes 73728 | tf_op jit(solution)/shard_map/all_gather | solution.py:158
  160.1 12.8 %all_gather.82 = bf16[8,32,128]{2,1,0:T(8,128)(2,1)S(1)} all-gather(bf16[1,32,128]{2,1,0:T(8,128)(2,1)S(1)} %copy.1443), channel_id=1, replica_groups=mesh['batch'=8,'tensor'=32] {'batch'}, dimensions={0}, use_global_device_ids=true | all-gather | bytes 73728 | tf_op jit(solution)/shard_map/all_gather | solution.py:158
  173.8 12.9 %all_gather.87 = bf16[8,32,128]{2,1,0:T(8,128)(2,1)S(1)} all-gather(bf16[1,32,128]{2,1,0:T(8,128)(2,1)S(1)} %copy.1470), channel_id=1, replica_groups=mesh['batch'=8,'tensor'=32] {'batch'}, dimensions={0}, use_global_device_ids=true | all-gather | bytes 73728 | tf_op jit(solution)/shard_map/all_gather | solution.py:158
  192.8 12.9 %all_gather.72 = bf16[8,32,128]{2,1,0:T(8,128)(2,1)S(1)} all-gather(bf16[1,32,128]{2,1,0:T(8,128)(2,1)} %copy.1387), channel_id=1, replica_groups=mesh['batch'=8,'tensor'=32] {'batch'}, dimensions={0}, use_global_device_ids=true | all-gather | bytes 73728 | tf_op jit(solution)/shard_map/all_gather | solution.py:158
  216.7 10.1 %gather_fusion = bf16[128,2,128,128]{3,2,1,0:T(8,128)(2,1)} fusion(bf16[128,2,128,128]{3,2,1,0:T(8,128)(2,1)} %all-gather.10.cloned.1.call-done, s32[1024]{0:T(1024)} %pad_clamp_fusion), kind=kCustom, calls=%fused_computation.10 | custom fusion | bytes 16777728 | tf_op jit(solution)/shard_map/gather | solution.py:127
  297.4 12.9 %all_gather.74 = f32[8,8,32,1]{2,1,3,0:T(8,128)S(1)} all-gather(f32[1,8,32,1]{2,1,3,0:T(8,128)S(1)} %get-tuple-element.1418), channel_id=1, replica_groups=mesh['batch'=8,'tensor'=32] {'batch'}, dimensions={0}, use_global_device_ids=true | all-gather | bytes 9216 | tf_op jit(solution)/shard_map/all_gather | solution.py:19
  310.3 12.9 %all_gather.73 = f32[8,8,32,1]{2,1,3,0:T(8,128)S(1)} all-gather(f32[1,8,32,1]{2,1,3,0:T(8,128)S(1)} %get-tuple-element.1419), channel_id=1, replica_groups=mesh['batch'=8,'tensor'=32] {'batch'}, dimensions={0}, use_global_device_ids=true | all-gather | bytes 9216 | tf_op jit(solution)/shard_map/all_gather | solution.py:19
  323.8 12.9 %all_gather.88 = f32[8,8,32,1]{2,1,3,0:T(8,128)S(1)} all-gather(f32[1,8,32,1]{2,1,3,0:T(8,128)S(1)} %get-tuple-element.1443), channel_id=1, replica_groups=mesh['batch'=8,'tensor'=32] {'batch'}, dimensions={0}, use_global_device_ids=true | all-gather | bytes 9216 | tf_op jit(solution)/shard_map/all_gather | solution.py:19
  336.7 12.9 %all_gather.89 = f32[8,8,32,1]{2,1,3,0:T(8,128)S(1)} all-gather(f32[1,8,32,1]{2,1,3,0:T(8,128)S(1)} %get-tuple-element.1444), channel_id=1, replica_groups=mesh['batch'=8,'tensor'=32] {'batch'}, dimensions={0}, use_global_device_ids=true | all-gather | bytes 9216 | tf_op jit(solution)/shard_map/all_gather | solution.py:19
  349.5 12.9 %all_gather.83 = f32[8,8,32,1]{2,1,3,0:T(8,128)S(1)} all-gather(f32[1,8,32,1]{2,1,3,0:T(8,128)S(1)} %get-tuple-element.1445), channel_id=1, replica_groups=mesh['batch'=8,'tensor'=32] {'batch'}, dimensions={0}, use_global_device_ids=true | all-gather | bytes 9216 | tf_op jit(solution)/shard_map/all_gather | solution.py:19
  363.0 12.9 %all_gather.84 = f32[8,8,32,1]{2,1,3,0:T(8,128)S(1)} all-gather(f32[1,8,32,1]{2,1,3,0:T(8,128)S(1)} %get-tuple-element.1446), channel_id=1, replica_groups=mesh['batch'=8,'tensor'=32] {'batch'}, dimensions={0}, use_global_device_ids=true | all-gather | bytes 9216 | tf_op jit(solution)/shard_map/all_gather | solution.py:19
  375.8 12.9 %all_gather.78 = f32[8,8,32,1]{2,1,3,0:T(8,128)S(1)} all-gather(f32[1,8,32,1]{2,1,3,0:T(8,128)S(1)} %get-tuple-element.1447), channel_id=1, replica_groups=mesh['batch'=8,'tensor'=32] {'batch'}, dimensions={0}, use_global_device_ids=true | all-gather | bytes 9216 | tf_op jit(solution)/shard_map/all_gather | solution.py:19
  388.7 12.9 %all_gather.79 = f32[8,8,32,1]{2,1,3,0:T(8,128)S(1)} all-gather(f32[1,8,32,1]{2,1,3,0:T(8,128)S(1)} %get-tuple-element.1448), channel_id=1, replica_groups=mesh['batch'=8,'tensor'=32] {'batch'}, dimensions={0}, use_global_device_ids=true | all-gather | bytes 9216 | tf_op jit(solution)/shard_map/all_gather | solution.py:19
  406.7 16.4 %while.84 = (s32[]{:T(128)}, f32[8,32,1]{1,2,0:T(1,128)S(1)}, f32[8,32,1]{1,2,0:T(1,128)S(1)}, f32[8,32,1,128]{3,2,1,0:T(1,128)S(1)}, f32[8,8,32,1]{2,1,3,0:T(8,...) while((s32[]{:T(128)}, f32[8,32,1]{1,2,0:T(1,128)S(1)}, ...), condition=%wide.region_7.9_spmd, body=%wide.region_6.8_spmd.sunk | while | flops 99845 | bytes 931983 | solution.py:24
  424.2 11.7 %while.85 = (s32[]{:T(128)}, f32[8,32,1]{1,2,0:T(1,128)S(1)}, f32[8,32,1]{1,2,0:T(1,128)S(1)}, f32[8,32,1,128]{3,2,1,0:T(1,128)S(1)}, f32[8,8,32,1]{2,1,3,0:T(8,...) while((s32[]{:T(128)}, f32[8,32,1]{1,2,0:T(1,128)S(1)}, ...), condition=%wide.region_16.18_spmd, body=%wide.region_15.17_spmd.sunk | while | flops 99845 | bytes 931983 | solution.py:24
  437.6 16.4 %while.87 = (s32[]{:T(128)}, f32[8,32,1]{1,2,0:T(1,128)S(1)}, f32[8,32,1]{1,2,0:T(1,128)S(1)}, f32[8,32,1,128]{3,2,1,0:T(1,128)S(1)}, f32[8,8,32,1]{2,1,3,0:T(8,...) while((s32[]{:T(128)}, f32[8,32,1]{1,2,0:T(1,128)S(1)}, ...), condition=%wide.region_34.36_spmd, body=%wide.region_33.35_spmd.sunk | while | flops 99845 | bytes 931983 | solution.py:24
  458.2 26.7 %while.86 = (s32[]{:T(128)}, f32[8,32,1]{1,2,0:T(1,128)S(1)}, f32[8,32,1]{1,2,0:T(1,128)S(1)}, f32[8,32,1,128]{3,2,1,0:T(1,128)}, f32[8,8,32,1]{2,1,3,0:T(8,128)...) while((s32[]{:T(128)}, f32[8,32,1]{1,2,0:T(1,128)S(1)}, ...), condition=%wide.region_25.27_spmd, body=%wide.region_24.26_spmd.sunk | while | flops 99845 | bytes 931983 | solution.py:24
  493.1 152.5 %all-reduce.9.cloned.1.call-done = (f32[32,1,4096]{2,0,1:T(8,128)}, f32[32,1,4096]{2,0,1:T(8,128)}, f32[32,1,4096]{2,0,1:T(8,128)}, f32[32,1,4096]{2,0,1:T(8,128)}) async-done(((f32[32,1,4096]{2,0,1:T(8,128)}, f32[32,1,4096]{2,0,1:T(8,128)}, f32[32,1,4096]{2,0,1:T(8,128)}, f32[32,1,4096]{2,0,1:T(8,128)}), (f32[32,1,4096]{2,0,1:T(8,128)}, f32[32,1,4096]{2,0,1:T(8,128)}, f32[32,1,4096]{2,0,1:T(8,128)}, ...) | async-done | bytes 2097168
  (589 shorter events, 273.0 us)
Async XLA Ops:
  6.5 242.0 %copy-start = (bf16[256,4096]{1,0:T(8,128)(2,1)S(1)}, bf16[256,4096]{1,0:T(8,128)(2,1)}, u32[]{:S(2)}) copy-start(bf16[256,4096]{1,0:T(8,128)(2,1)} %param.47) | copy-start | bytes 6291460
  6.5 210.1 %all-gather.10.cloned.1.call-start = ((), (), s32[]{:S(2)}) async-start(), calls=%async_computation.4 | async-start | bytes 9437184 | tf_op jit(solution)/shard_map/all_gather | solution.py:126
  21.8 54.0 %all-to-all-start.3 = ((bf16[32,2,2048]{2,1,0:T(2,128)(2,1)}), bf16[32,2,2048]{2,1,0:T(2,128)(2,1)S(1)}, u32[]{:S(2)}, u32[]{:S(2)}) async-start(bf16[32,2,2048]{2,1,0:T(2,128)(2,1)} %reshape.4169), calls=%async_computation.3 | async-start | bytes 524288 | tf_op jit(solution)/shard_map/all_to_all | solution.py:136
  75.7 21.7 %all-to-all-start.2 = ((bf16[32,2,2048]{2,1,0:T(2,128)(2,1)}), bf16[32,2,2048]{2,1,0:T(2,128)(2,1)S(1)}, u32[]{:S(2)}, u32[]{:S(2)}) async-start(bf16[32,2,2048]{2,1,0:T(2,128)(2,1)} %reshape.4175), calls=%async_computation.2 | async-start | bytes 524288 | tf_op jit(solution)/shard_map/all_to_all | solution.py:136
  97.5 15.8 %all-to-all-start.1 = ((bf16[32,2,2048]{2,1,0:T(2,128)(2,1)}), bf16[32,2,2048]{2,1,0:T(2,128)(2,1)S(1)}, u32[]{:S(2)}, u32[]{:S(2)}) async-start(bf16[32,2,2048]{2,1,0:T(2,128)(2,1)} %reshape.4173), calls=%async_computation.1 | async-start | bytes 524288 | tf_op jit(solution)/shard_map/all_to_all | solution.py:136
  114.0 16.9 %all-to-all-start = ((bf16[32,2,2048]{2,1,0:T(2,128)(2,1)}), bf16[32,2,2048]{2,1,0:T(2,128)(2,1)S(1)}, u32[]{:S(2)}, u32[]{:S(2)}) async-start(bf16[32,2,2048]{2,1,0:T(2,128)(2,1)} %reshape.4171), calls=%async_computation | async-start | bytes 524288 | tf_op jit(solution)/shard_map/all_to_all | solution.py:136
  119.2 286.5 %all-gather.12.cloned.1.call-start = ((), (), s32[]{:S(2)}) async-start(), calls=%async_computation.5 | async-start | bytes 1179648 | tf_op jit(solution)/shard_map/all_gather | solution.py:19
  187.4 21.0 %collective-permute-start.7 = (f32[8,32,1,1,68]{4,0,1,3,2:T(8,128)S(1)}, f32[8,32,1,1,68]{4,0,1,3,2:T(8,128)S(1)}, u32[]{:S(2)}, u32[]{:S(2)}) collective-permute-start(f32[8,32,1,1,68]{4,0,1,3,2:T(8,128)S(1)} %maximum_multiply_fusion.3), channel_id=1, source_target_pairs={{0,1},{1,0},{2,3},{3,2},{4,5},{5,4},{6,7},{7,6},{8,9},{9,8},{10,11... | collective-permute-start | bytes 208904 | tf_op jit(solution)/shard_map/ppermute | solution.py:15
  190.1 20.6 %collective-permute-start.5 = (f32[8,32,1,1,68]{4,0,1,3,2:T(8,128)S(1)}, f32[8,32,1,1,68]{4,0,1,3,2:T(8,128)S(1)}, u32[]{:S(2)}, u32[]{:S(2)}) collective-permute-start(f32[8,32,1,1,68]{4,0,1,3,2:T(8,128)S(1)} %maximum_multiply_fusion.2), channel_id=1, source_target_pairs={{0,1},{1,0},{2,3},{3,2},{4,5},{5,4},{6,7},{7,6},{8,9},{9,8},{10,11... | collective-permute-start | bytes 208904 | tf_op jit(solution)/shard_map/ppermute | solution.py:15
  191.4 48.5 %collective-permute-start.3 = (f32[8,32,1,1,68]{4,0,1,3,2:T(8,128)S(1)}, f32[8,32,1,1,68]{4,0,1,3,2:T(8,128)}, u32[]{:S(2)}, u32[]{:S(2)}) collective-permute-start(f32[8,32,1,1,68]{4,0,1,3,2:T(8,128)S(1)} %maximum_multiply_fusion.1), channel_id=1, source_target_pairs={{0,1},{1,0},{2,3},{3,2},{4,5},{5,4},{6,7},{7,6},{8,9},{9,8},{10,11... | collective-permute-start | bytes 208904 | tf_op jit(solution)/shard_map/ppermute | solution.py:15
  206.4 6.7 %collective-permute-start.1 = (f32[8,32,1,1,68]{4,0,1,3,2:T(8,128)S(1)}, f32[8,32,1,1,68]{4,0,1,3,2:T(8,128)S(1)}, u32[]{:S(2)}, u32[]{:S(2)}) collective-permute-start(f32[8,32,1,1,68]{4,0,1,3,2:T(8,128)S(1)} %maximum_multiply_fusion), channel_id=1, source_target_pairs={{0,1},{1,0},{2,3},{3,2},{4,5},{5,4},{6,7},{7,6},{8,9},{9,8},{10,11... | collective-permute-start | bytes 208904 | tf_op jit(solution)/shard_map/ppermute | solution.py:15
  235.8 5.4 collective-permute-start.6
  237.2 5.0 collective-permute-start.4
  237.9 5.7 collective-permute-start.2
  239.2 5.2 collective-permute-start
  248.5 174.7 %all-gather.14.cloned.1.call-start = ((), (), s32[]{:S(2)}) async-start(), calls=%async_computation.6 | async-start | bytes 1179648 | tf_op jit(solution)/shard_map/all_gather | solution.py:19
  264.2 171.9 %all-gather.18.cloned.1.call-start = ((), (), s32[]{:S(2)}) async-start(), calls=%async_computation.8 | async-start | bytes 1179648 | tf_op jit(solution)/shard_map/all_gather | solution.py:19
  277.8 178.7 %all-gather.16.cloned.1.call-start = ((), (), s32[]{:S(2)}) async-start(), calls=%async_computation.7 | async-start | bytes 1179648 | tf_op jit(solution)/shard_map/all_gather | solution.py:19
  292.0 112.4 %copy-start.27 = (bf16[8,32,1,1,68]{4,0,1,3,2:T(8,128)(2,1)S(1)}, bf16[8,32,1,1,68]{4,0,1,3,2:T(8,128)(2,1)}, u32[]{:S(2)}) copy-start(bf16[8,32,1,1,68]{4,0,1,3,2:T(8,128)(2,1)} %copy-done.26) | copy-start | bytes 104452
  294.0 110.4 %copy-start.37 = (f32[32,128,8]{1,2,0:T(8,128)S(1)}, f32[32,128,8]{1,2,0:T(8,128)}, u32[]{:S(2)}) copy-start(f32[32,128,8]{1,2,0:T(8,128)} %fusion.57) | copy-start | bytes 393220
  296.6 107.8 %copy-start.67 = (pred[8]{0:T(512)(128)(4,1)S(1)}, pred[8]{0:T(512)(128)(4,1)}, u32[]{:S(2)}) copy-start(pred[8]{0:T(512)(128)(4,1)} %iota_compare_fusion.2) | copy-start | bytes 28
  405.4 240.2 %all-reduce.9.cloned.1.call-start = ((), (), s32[]{:S(2)}) async-start(), calls=%async_computation.9 | async-start | bytes 4194304
  489.4 156.1 %copy-start.5 = (bf16[4,1,1,4096]{3,0,2,1:T(4,128)(2,1)S(1)}, bf16[4,1,1,4096]{3,0,2,1:T(4,128)(2,1)}, u32[]{:S(2)}) copy-start(bf16[4,1,1,4096]{3,0,2,1:T(4,128)(2,1)} %param.40) | copy-start | bytes 98308
  489.4 156.1 %copy-start.57 = (f32[4096]{0:T(1024)S(1)}, f32[4096]{0:T(1024)}, u32[]{:S(2)}) copy-start(f32[4096]{0:T(1024)} %param.48) | copy-start | bytes 49156
  (66 other events, 944.4 us)
Sparse Core Ops, SparseCore 0:
  9.2 54.3 all-gather.9
  248.6 23.0 all-gather.11
  273.6 26.7 all-gather.13
  302.1 26.8 all-gather.17
  405.5 23.1 all-gather.15
  492.6 152.9 all-reduce.8
